TPU v7x, 32 devices: a whole 2x2x4 slice. The times are simulated.
32 devices in a mesh: groups: 2 (over x), ex: 16 (over z, y, core).
Axes of the slice: x: 2, y: 2, z: 4, core: 2. Of those that a mesh axis runs over, the one named last changes fastest.
Arguments:
- grads: bfloat16 [1024, 65536], P(('groups', 'ex')), parts along dimension 0, may hold values from -6 to 6
- proj: bfloat16 [65536, 1024], P('ex'), may hold values from -0.0234375 to 0.0234375
- target_ids: int32 [24, 128], replicated, may hold values from 0 to 511, as said below
- target_counts: int32 [24], replicated, may hold values from 1 to 128, as said below
Outputs:
- scores: float32 [1024, 24], P(('groups', 'ex')), parts along dimension 0
- sketch: float32 [1024, 1024], P(('groups', 'ex')), parts along dimension 0
There are 2 independent parts, one for each index of `groups`. A program takes and returns all parts, laid end to end along the dimension named above; an argument that names none is the same for every part. Nothing has to cross between parts.
Inputs may be any that keep to these rules, and one draw needn't show every extreme that they name: `target_ids`: indices of examples of this part; slots at or past a domain's count are ignored. `target_counts`: some domain fills all 128 slots.
All inputs are finite; a program needn't handle non-finite values.
Results may differ from a plain program's by a relative error of at most 0.0003.
Values may be sent and summed in bfloat16 or wider, within the bound.
No kernel may reach another device: no remote copies, remote signals or barrier semaphores. Data moves between devices by JAX's collectives and lax.ppermute only.
A program may use at most 128 MiB of HBM per device.

v0:
```python
import jax
import jax.numpy as jnp
from jax import lax
from jax.sharding import PartitionSpec as P


def partner(array, axis, bit):
    return lax.ppermute(array, axis, [(i, i ^ 1 << bit) for i in range(lax.axis_size(axis))])


def reduce_scatter(partial_value, bits, position):
    value = partial_value
    for level in range(bits):
        value = value.reshape((-1, 2) + value.shape[1:])
        own_bit = position // 2**level % 2
        kept = lax.dynamic_index_in_dim(value, own_bit, axis=1, keepdims=False)
        sent = lax.dynamic_index_in_dim(value, 1 - own_bit, axis=1, keepdims=False)
        value = kept + partner(sent, "ex", level)
    return value[0]


def all_gather(block, bits, position):
    value = block[None]
    for level in range(bits - 1, -1, -1):
        received = partner(value, "ex", level)
        high_side = position // 2**level % 2 == 1
        low = jnp.where(high_side, received, value)
        high = jnp.where(high_side, value, received)
        value = jnp.stack([low, high], axis=1).reshape((-1,) + value.shape[1:])
    return value


def on_device(grads, proj, target_ids, target_counts):
    count_ex = lax.axis_size("ex")
    bits = count_ex.bit_length() - 1
    position = lax.axis_index("ex")
    ex_rows = grads.shape[0]
    examples = ex_rows * count_ex
    sketch_width = proj.shape[1]
    with jax.named_scope("gradient_exchange"):
        columns = lax.all_to_all(grads, "ex", split_axis=1, concat_axis=0, tiled=True)
    with jax.named_scope("partial_projection"):
        partial_value = jnp.dot(columns, proj, preferred_element_type=jnp.float32)
    with jax.named_scope("sketch_reduce"):
        sketch = reduce_scatter(
            partial_value.reshape(count_ex, ex_rows, sketch_width), bits, position
        )
    with jax.named_scope("sketch_gather"):
        sketch_all = all_gather(sketch, bits, position).reshape(examples, sketch_width)
    slot_count = target_ids.shape[1]
    live_slot = jnp.arange(slot_count, dtype=jnp.int32)[None, :] < target_counts[:, None]
    example_index = jnp.arange(examples, dtype=jnp.int32)
    matches = (target_ids[:, :, None] == example_index[None, None, :]) & live_slot[:, :, None]
    weight = jnp.sum(matches.astype(jnp.float32), axis=1) / target_counts[:, None].astype(
        jnp.float32
    )
    if examples < sketch_width:
        with jax.named_scope("kernel_matrix"):
            kernel = jnp.dot(sketch_all, sketch_all.T, precision=lax.Precision.HIGHEST)
        with jax.named_scope("kernel_solve"):
            system = kernel / jnp.float32(examples) + 0.1 * jnp.eye(examples, dtype=jnp.float32)
            factor = jnp.linalg.cholesky(system)
            middle = lax.linalg.triangular_solve(factor, weight.T, left_side=True, lower=True)
            coeffs = lax.linalg.triangular_solve(
                factor, middle, left_side=True, lower=True, transpose_a=True
            )
        own_kernel = lax.dynamic_slice_in_dim(kernel, position * ex_rows, ex_rows, axis=0)
        scores = jnp.dot(own_kernel, coeffs, precision=lax.Precision.HIGHEST)
    else:
        with jax.named_scope("gram_solve"):
            gram_matrix = jnp.dot(sketch_all.T, sketch_all, precision=lax.Precision.HIGHEST)
            domain = jnp.dot(weight, sketch_all, precision=lax.Precision.HIGHEST)
            hessian = gram_matrix / jnp.float32(examples) + 0.1 * jnp.eye(
                sketch_width, dtype=jnp.float32
            )
            factor = jnp.linalg.cholesky(hessian)
            middle = lax.linalg.triangular_solve(factor, domain.T, left_side=True, lower=True)
            solved = lax.linalg.triangular_solve(
                factor, middle, left_side=True, lower=True, transpose_a=True
            )
        scores = jnp.dot(sketch, solved, precision=lax.Precision.HIGHEST)
    return (scores, sketch)


def solution(mesh):
    placed = (P(("groups", "ex"), None), P("ex", None), P(), P())
    return jax.shard_map(
        on_device,
        mesh=mesh,
        in_specs=placed,
        out_specs=(P(("groups", "ex"), None), P(("groups", "ex"), None)),
        check_vma=False,
    )
```

profile of v0, /device:TPU:0, one launch (start us, length us, event | category | flops | bytes accessed | tf_op | source)
XLA Modules:
  0.0 324.4 jit_solution(8416492365125750362)
XLA Ops:
  0.6 4.7 %copy.26 = bf16[4,16,8,4096]{3,2,0,1:T(8,128)(2,1)} copy(bf16[4,16,8,4096]{3,2,1,0:T(8,128)(2,1)} %bitcast.121) | data formatting | bytes 8388608 | tf_op jit(solution)/shard_map/gradient_exchange/all_to_all | solution.py:41
  5.3 7.4 %all-to-all-start = ((bf16[32,16,4096]{2,0,1:T(8,128)(2,1)}), bf16[32,16,4096]{2,0,1:T(8,128)(2,1)}, u32[]{:S(2)}, u32[]{:S(2)}) async-start(bf16[32,16,4096]{2,0,1:T(8,128)(2,1)} %bitcast.119), calls=%async_computation | async-start | bytes 8388608 | tf_op jit(solution)/shard_map/gradient_exchange/all_to_all | solution.py:41
  12.7 77.7 %all-to-all-done = bf16[32,16,4096]{2,0,1:T(8,128)(2,1)} async-done(((bf16[32,16,4096]{2,0,1:T(8,128)(2,1)}), bf16[32,16,4096]{2,0,1:T(8,128)(2,1)}, u32[]{:S(2)}, u32[]{:S(2)}) %all-to-all-start) | async-done | bytes 4194336 | tf_op jit(solution)/shard_map/gradient_exchange/all_to_all | solution.py:41
  90.4 8.1 %fusion = f32[8,2,32,1024]{3,2,1,0:T(8,128)S(1)} fusion(bf16[8,2,32,4096]{3,2,1,0:T(8,128)(2,1)} %bitcast.1, bf16[4096,1024]{1,0:T(8,128)(2,1)} %param.5), kind=kOutput, calls=%fused_computation.2 | convolution fusion | flops 4294967296 | bytes 14680064 | tf_op jit(solution)/shard_map/partial_projection/dot_general | solution.py:43
  98.7 0.8 collective-permute-start
  99.5 2.4 collective-permute-done
  101.9 1.4 bitcast_add_fusion
  103.3 6.3 %collective-permute-start.1 = (f32[4,32,1024]{2,1,0:T(8,128)S(1)}, f32[4,32,1024]{2,1,0:T(8,128)S(1)}, u32[]{:S(2)}, u32[]{:S(2)}) collective-permute-start(f32[4,32,1024]{2,1,0:T(8,128)S(1)} %dynamic-slice_bitcast_fusion.1), channel_id=1, source_target_pairs={{0,2},{1,3},{2,0},{3,1},{4,6},{5,7},{6,4},{7,5},{8,10},{9,11},{10,... | collective-permute-start | bytes 1572872 | tf_op jit(solution)/shard_map/sketch_reduce/ppermute | solution.py:8
  109.6 12.4 %collective-permute-done.1 = f32[4,32,1024]{2,1,0:T(8,128)S(1)} collective-permute-done((f32[4,32,1024]{2,1,0:T(8,128)S(1)}, f32[4,32,1024]{2,1,0:T(8,128)S(1)}, u32[]{:S(2)}, u32[]{:S(2)}) %collective-permute-start.1) | collective-permute-done | bytes 524320 | tf_op jit(solution)/shard_map/sketch_reduce/ppermute | solution.py:8
  122.2 11.4 %collective-permute-start.2 = (f32[2,32,1024]{2,1,0:T(8,128)S(1)}, f32[2,32,1024]{2,1,0:T(8,128)S(1)}, u32[]{:S(2)}, u32[]{:S(2)}) collective-permute-start(f32[2,32,1024]{2,1,0:T(8,128)S(1)} %dynamic-slice_bitcast_fusion.2), channel_id=1, source_target_pairs={{0,4},{1,5},{2,6},{3,7},{4,0},{5,1},{6,2},{7,3},{8,12},{9,13},{10,... | collective-permute-start | bytes 786440 | tf_op jit(solution)/shard_map/sketch_reduce/ppermute | solution.py:8
  133.6 6.3 %collective-permute-done.2 = f32[2,32,1024]{2,1,0:T(8,128)S(1)} collective-permute-done((f32[2,32,1024]{2,1,0:T(8,128)S(1)}, f32[2,32,1024]{2,1,0:T(8,128)S(1)}, u32[]{:S(2)}, u32[]{:S(2)}) %collective-permute-start.2) | collective-permute-done | bytes 262176 | tf_op jit(solution)/shard_map/sketch_reduce/ppermute | solution.py:8
  139.9 2.7 collective-permute-start.3
  142.6 5.7 %collective-permute-done.3 = f32[1,32,1024]{2,1,0:T(8,128)S(1)} collective-permute-done((f32[1,32,1024]{2,1,0:T(8,128)S(1)}, f32[1,32,1024]{2,1,0:T(8,128)S(1)}, u32[]{:S(2)}, u32[]{:S(2)}) %collective-permute-start.3) | collective-permute-done | bytes 131104 | tf_op jit(solution)/shard_map/sketch_reduce/ppermute | solution.py:8
  148.4 0.3 collective-permute-start.4
  148.7 7.9 %collective-permute-done.4 = f32[1,32,1024]{2,1,0:T(8,128)S(1)} collective-permute-done((f32[1,32,1024]{2,1,0:T(8,128)S(1)}, f32[1,32,1024]{2,1,0:T(8,128)S(1)}, u32[]{:S(2)}, u32[]{:S(2)}) %collective-permute-start.4) | collective-permute-done | bytes 131104 | tf_op jit(solution)/shard_map/sketch_gather/ppermute | solution.py:8
  156.7 8.2 %collective-permute-done.5 = f32[2,32,1024]{2,1,0:T(8,128)S(1)} collective-permute-done((f32[2,32,1024]{2,1,0:T(8,128)S(1)}, f32[2,32,1024]{2,1,0:T(8,128)S(1)}, u32[]{:S(2)}, u32[]{:S(2)}) %collective-permute-start.5) | collective-permute-done | bytes 262176 | tf_op jit(solution)/shard_map/sketch_gather/ppermute | solution.py:8
  165.1 13.0 %collective-permute-done.6 = f32[4,32,1024]{2,1,0:T(8,128)S(1)} collective-permute-done((f32[4,32,1024]{2,1,0:T(8,128)S(1)}, f32[4,32,1024]{2,1,0:T(8,128)S(1)}, u32[]{:S(2)}, u32[]{:S(2)}) %collective-permute-start.6) | collective-permute-done | bytes 524320 | tf_op jit(solution)/shard_map/sketch_gather/ppermute | solution.py:8
  178.5 0.4 copy-done.2
  178.9 2.0 convert_reduce_fusion
  181.1 0.2 select_bitcast_fusion.1
  181.4 0.2 pad_maximum_fusion
  181.6 0.2 copy.21
  181.9 3.5 %fusion.61 = f32[512,512]{1,0:T(8,128)S(1)} fusion(f32[512,1024]{1,0:T(8,128)S(1)} %bitcast.118), kind=kOutput, calls=%fused_computation.127 | convolution fusion | flops 3221225472 | bytes 3145728 | tf_op jit(solution)/shard_map/kernel_matrix/dot_general | solution.py:59
  185.5 0.3 copy.22
  185.9 0.2 add_multiply_fusion
  186.1 11.7 %cholesky.103 = f32[128,128]{1,0:T(8,128)S(1)} custom-call(f32[128,128]{1,0:T(8,128)S(1)} %cholesky.263), custom_call_target="Cholesky" | custom-call | tf_op jit(solution)/shard_map/kernel_solve/jit(cholesky)/cholesky | solution.py:62
  198.0 9.8 %custom-call.32 = f32[1,128,128]{1,2,0:T(8,128)S(1)} custom-call(f32[1,128,128]{2,1,0:T(8,128)S(1)} %get-tuple-element.37), custom_call_target="InvertDiagBlocksLowerTriangular" | custom-call | tf_op jit(solution)/shard_map/kernel_solve/jit(cholesky)/cholesky | solution.py:62
  207.8 0.3 constant_dynamic-update-slice_fusion
  208.1 0.3 convolution_subtract_fusion
  208.5 11.9 %cholesky.215 = f32[128,128]{1,0:T(8,128)S(1)} custom-call(f32[128,128]{1,0:T(8,128)S(1)} %cholesky.267), custom_call_target="Cholesky" | custom-call | tf_op jit(solution)/shard_map/kernel_solve/jit(cholesky)/cholesky | solution.py:62
  220.4 9.8 %custom-call.33 = f32[1,128,128]{1,2,0:T(8,128)S(1)} custom-call(f32[1,128,128]{2,1,0:T(8,128)S(1)} %get-tuple-element.34), custom_call_target="InvertDiagBlocksLowerTriangular" | custom-call | tf_op jit(solution)/shard_map/kernel_solve/jit(cholesky)/cholesky | solution.py:62
  230.2 0.3 convolution_dynamic-update-slice_fusion
  230.5 0.4 convolution_subtract_fusion.1
  230.9 11.7 %cholesky.236 = f32[128,128]{1,0:T(8,128)S(1)} custom-call(f32[128,128]{1,0:T(8,128)S(1)} %cholesky.272), custom_call_target="Cholesky" | custom-call | tf_op jit(solution)/shard_map/kernel_solve/jit(cholesky)/cholesky | solution.py:62
  242.6 9.8 %custom-call.34 = f32[1,128,128]{1,2,0:T(8,128)S(1)} custom-call(f32[1,128,128]{2,1,0:T(8,128)S(1)} %get-tuple-element.31), custom_call_target="InvertDiagBlocksLowerTriangular" | custom-call | tf_op jit(solution)/shard_map/kernel_solve/jit(cholesky)/cholesky | solution.py:62
  252.5 0.2 convolution_dynamic-update-slice_fusion.1
  252.7 0.6 convolution_subtract_fusion.2
  253.3 11.7 %cholesky.253 = f32[128,128]{1,0:T(8,128)S(1)} custom-call(f32[128,128]{1,0:T(8,128)S(1)} %convolution_subtract_fusion.2), custom_call_target="Cholesky" | custom-call | tf_op jit(solution)/shard_map/kernel_solve/jit(cholesky)/cholesky | solution.py:62
  265.0 0.7 compare_reduce_fusion.1
  265.7 0.7 compare_reduce_fusion
  266.4 0.7 compare_reduce_fusion.2
  269.7 10.5 %while.1 = (s32[]{:T(128)}, f32[512,512]{1,0:T(8,128)S(1)}, s32[4,2]{0,1:T(2,128)S(1)}, f32[4,128,128]{2,1,0:T(8,128)}, s32[]{:T(128)}) while((s32[]{:T(128)}, f32[512,512]{1,0:T(8,128)S(1)}, s32[4,2]{0,1:T(2,128)S(1)}, f32[4,128,128]{2,1,0:T(8,128)}, s32[]{:T(128)}) %tuple.35), condition=%wide.while_cond, body=%wide.while_body.sunk | while | flops 2 | bytes 132205 | solution.py:64
  269.8 0.6 fusion.76
  270.4 2.0 bitcast_dynamic-update-slice_fusion.2
  272.4 0.6 fusion.76
  273.0 2.0 bitcast_dynamic-update-slice_fusion.2
  275.1 0.6 fusion.76
  275.6 2.0 bitcast_dynamic-update-slice_fusion.2
  277.7 0.6 fusion.76
  278.3 2.0 bitcast_dynamic-update-slice_fusion.2
  280.2 40.1 %custom-call.35 = f32[4,128,128]{1,2,0:T(8,128)S(1)} custom-call(f32[4,128,128]{2,1,0:T(8,128)} %get-tuple-element.9), custom_call_target="InvertDiagBlocksLowerTriangular" | custom-call | tf_op jit(solution)/shard_map/kernel_solve/triangular_solve | solution.py:64
  320.5 0.2 convolution_subtract_fusion.8
  320.7 0.2 fusion.25
  320.9 0.2 convolution_subtract_fusion.7
  321.3 0.3 convolution_subtract_fusion.6
  321.6 0.2 fusion.29
  321.8 0.2 fusion.28
  322.1 0.2 convolution_subtract_fusion.5
  322.3 0.2 fusion.26
  322.5 0.2 convolution_subtract_fusion.4
  322.7 0.2 fusion.24
  322.9 0.3 convolution_subtract_fusion.3
  323.2 0.2 fusion.22
  323.4 0.8 fusion.20
  (45 shorter events, 2.4 us)
Async XLA Ops:
  5.3 85.1 %all-to-all-start = ((bf16[32,16,4096]{2,0,1:T(8,128)(2,1)}), bf16[32,16,4096]{2,0,1:T(8,128)(2,1)}, u32[]{:S(2)}, u32[]{:S(2)}) async-start(bf16[32,16,4096]{2,0,1:T(8,128)(2,1)} %bitcast.119), calls=%async_computation | async-start | bytes 8388608 | tf_op jit(solution)/shard_map/gradient_exchange/all_to_all | solution.py:41
  98.7 3.3 %collective-permute-start = (f32[8,32,1024]{2,1,0:T(8,128)S(1)}, f32[8,32,1024]{2,1,0:T(8,128)}, u32[]{:S(2)}, u32[]{:S(2)}) collective-permute-start(f32[8,32,1024]{2,1,0:T(8,128)S(1)} %dynamic-slice_bitcast_fusion), channel_id=1, source_target_pairs={{0,1},{1,0},{2,3},{3,2},{4,5},{5,4},{6,7},{7,6},{8,9},{9,8},{10,11... | collective-permute-start | bytes 3145736 | tf_op jit(solution)/shard_map/sketch_reduce/ppermute | solution.py:8
  103.3 18.7 %collective-permute-start.1 = (f32[4,32,1024]{2,1,0:T(8,128)S(1)}, f32[4,32,1024]{2,1,0:T(8,128)S(1)}, u32[]{:S(2)}, u32[]{:S(2)}) collective-permute-start(f32[4,32,1024]{2,1,0:T(8,128)S(1)} %dynamic-slice_bitcast_fusion.1), channel_id=1, source_target_pairs={{0,2},{1,3},{2,0},{3,1},{4,6},{5,7},{6,4},{7,5},{8,10},{9,11},{10,... | collective-permute-start | bytes 1572872 | tf_op jit(solution)/shard_map/sketch_reduce/ppermute | solution.py:8
  122.2 17.7 %collective-permute-start.2 = (f32[2,32,1024]{2,1,0:T(8,128)S(1)}, f32[2,32,1024]{2,1,0:T(8,128)S(1)}, u32[]{:S(2)}, u32[]{:S(2)}) collective-permute-start(f32[2,32,1024]{2,1,0:T(8,128)S(1)} %dynamic-slice_bitcast_fusion.2), channel_id=1, source_target_pairs={{0,4},{1,5},{2,6},{3,7},{4,0},{5,1},{6,2},{7,3},{8,12},{9,13},{10,... | collective-permute-start | bytes 786440 | tf_op jit(solution)/shard_map/sketch_reduce/ppermute | solution.py:8
  139.9 8.4 %collective-permute-start.3 = (f32[1,32,1024]{2,1,0:T(8,128)S(1)}, f32[1,32,1024]{2,1,0:T(8,128)S(1)}, u32[]{:S(2)}, u32[]{:S(2)}) collective-permute-start(f32[1,32,1024]{2,1,0:T(8,128)S(1)} %constant_dynamic-slice_fusion.1), channel_id=1, source_target_pairs={{0,8},{1,9},{2,10},{3,11},{4,12},{5,13},{6,14},{7,15},{8,0},{9,1},... | collective-permute-start | bytes 393224 | tf_op jit(solution)/shard_map/sketch_reduce/ppermute | solution.py:8
  148.3 29.9 %copy-start = (f32[1,32,1024]{2,1,0:T(8,128)}, f32[1,32,1024]{2,1,0:T(8,128)S(1)}, u32[]{:S(2)}) copy-start(f32[1,32,1024]{2,1,0:T(8,128)S(1)} %dynamic-slice_add_fusion) | copy-start | bytes 393220
  148.4 8.2 %collective-permute-start.4 = (f32[1,32,1024]{2,1,0:T(8,128)S(1)}, f32[1,32,1024]{2,1,0:T(8,128)S(1)}, u32[]{:S(2)}, u32[]{:S(2)}) collective-permute-start(f32[1,32,1024]{2,1,0:T(8,128)S(1)} %dynamic-slice_add_fusion), channel_id=1, source_target_pairs={{0,8},{1,9},{2,10},{3,11},{4,12},{5,13},{6,14},{7,15},{8,0},{9,1},... | collective-permute-start | bytes 393224 | tf_op jit(solution)/shard_map/sketch_gather/ppermute | solution.py:8
  156.6 8.3 %collective-permute-start.5 = (f32[2,32,1024]{2,1,0:T(8,128)S(1)}, f32[2,32,1024]{2,1,0:T(8,128)S(1)}, u32[]{:S(2)}, u32[]{:S(2)}) collective-permute-start(f32[2,32,1024]{2,1,0:T(8,128)S(1)} %maximum_bitcast_fusion), channel_id=1, source_target_pairs={{0,4},{1,5},{2,6},{3,7},{4,0},{5,1},{6,2},{7,3},{8,12},{9,13},{10,... | collective-permute-start | bytes 786440 | tf_op jit(solution)/shard_map/sketch_gather/ppermute | solution.py:8
  165.0 13.1 %collective-permute-start.6 = (f32[4,32,1024]{2,1,0:T(8,128)S(1)}, f32[4,32,1024]{2,1,0:T(8,128)S(1)}, u32[]{:S(2)}, u32[]{:S(2)}) collective-permute-start(f32[4,32,1024]{2,1,0:T(8,128)S(1)} %bitcast.124), channel_id=1, source_target_pairs={{0,2},{1,3},{2,0},{3,1},{4,6},{5,7},{6,4},{7,5},{8,10},{9,11},{10,... | collective-permute-start | bytes 1572872 | tf_op jit(solution)/shard_map/sketch_gather/ppermute | solution.py:8
  178.2 0.7 copy-start.2
  178.2 0.7 copy-start.1
  178.4 2.7 collective-permute-start.7
where the time goes:
time: 328 us; the launch traced here: 324 us
  waiting for transfers between devices  134 us (41%)
  other arithmetic  124 us (38%)
  starting transfers between devices  29.1 us (9%)
  matrix products  17.5 us (5%)
  local copies, waits for them, and re-layouts  16.5 us (5%)
  between operations  3.86 us (1%)
    another operation x14, other arithmetic, on_device(): factor = jnp.linalg.cholesky(system)  78.7 us
    all_to_all x1, waiting for transfers between devices, on_device(): lax.all_to_all(grads, 'ex', split_axis=1, concat_axis=0, tiled=True)  77.7 us
    ppermute x8, waiting for transfers between devices, partner(): lax.ppermute(array, axis, [(i, i ^ 1 << bit) for i in range(lax.axis_size...  56.1 us
    another operation x3, other arithmetic, on_device(): lax.linalg.triangular_solve(factor, middle, left_side=True, lower=True, t...  40.2 us
    ppermute x8, starting transfers between devices, partner(): lax.ppermute(array, axis, [(i, i ^ 1 << bit) for i in range(lax.axis_size...  21.7 us
    another operation x12, local copies, waits for them, and re-layouts  10.5 us
    dot_general x1, matrix products, on_device(): partial_value = jnp.dot(columns, proj, preferred_element_type=jnp.float32)  8.14 us
    all_to_all x1, starting transfers between devices, on_device(): lax.all_to_all(grads, 'ex', split_axis=1, concat_axis=0, tiled=True)  7.44 us
  transfers between devices with their start and end apart: 9, of which 9 were waited for; matrix products, arithmetic and copies ran while one was open for 1% of the time, Pallas kernels for 0%

commit v1 on v0

--- a/solution.py
+++ b/solution.py
@@ -38,7 +38,10 @@
     examples = ex_rows * count_ex
     sketch_width = proj.shape[1]
     with jax.named_scope("gradient_exchange"):
-        columns = lax.all_to_all(grads, "ex", split_axis=1, concat_axis=0, tiled=True)
+        columns = jnp.concatenate(
+            lax.all_to_all(jnp.stack(jnp.split(grads, lax.axis_size("ex"), axis=1)), "ex", 0, 0),
+            axis=0,
+        )
     with jax.named_scope("partial_projection"):
         partial_value = jnp.dot(columns, proj, preferred_element_type=jnp.float32)
     with jax.named_scope("sketch_reduce"):

time: 328 us -> 351 us (1.070)
  local copies, waits for them, and re-layouts: 16.5 us -> 38.3 us
    unnamed x6 -> x21, local copies, waits for them, and re-layouts: 0.37 us -> 25.1 us
    all_to_all x1 -> x0, local copies, waits for them, and re-layouts: 4.66 us -> none  [on_device(): lax.all_to_all(grads, 'ex', split_axis=1, concat_axis=0, tiled=True)]
    another operation x12 -> x13, local copies, waits for them, and re-layouts: 10.5 us -> 12.2 us
where the time goes in v1:
time: 351 us; the launch traced here: 347 us
  waiting for transfers between devices  134 us (38%)
  other arithmetic  124 us (35%)
  local copies, waits for them, and re-layouts  38.3 us (11%)
  starting transfers between devices  29.1 us (8%)
  matrix products  17.5 us (5%)
  between operations  3.89 us (1%)
    another operation x14, other arithmetic, on_device(): factor = jnp.linalg.cholesky(system)  78.7 us
    all_to_all x1, waiting for transfers between devices, on_device(): lax.all_to_all(jnp.stack(jnp.split(grads, lax.axis_size('ex'), axis=1)),...  77.7 us
    ppermute x8, waiting for transfers between devices, partner(): lax.ppermute(array, axis, [(i, i ^ 1 << bit) for i in range(lax.axis_size...  56.4 us
    another operation x3, other arithmetic, on_device(): lax.linalg.triangular_solve(factor, middle, left_side=True, lower=True, t...  40.3 us
    unnamed x21, local copies, waits for them, and re-layouts  25.1 us
    ppermute x8, starting transfers between devices, partner(): lax.ppermute(array, axis, [(i, i ^ 1 << bit) for i in range(lax.axis_size...  21.7 us
    another operation x12, local copies, waits for them, and re-layouts  10.5 us
    dot_general x1, matrix products, on_device(): partial_value = jnp.dot(columns, proj, preferred_element_type=jnp.float32)  8.14 us
  transfers between devices with their start and end apart: 9, of which 9 were waited for; matrix products, arithmetic and copies ran while one was open for 1% of the time, Pallas kernels for 0%

profile of v1, /device:TPU:0, one launch (start us, length us, event | category | flops | bytes accessed | tf_op | source)
XLA Modules:
  0.0 346.5 jit_solution(18422283665668879057)
XLA Ops:
  0.6 1.7 bitcast_dynamic-update-slice_fusion.16
  2.3 1.7 bitcast_dynamic-update-slice_fusion.15
  4.0 1.7 bitcast_dynamic-update-slice_fusion.14
  5.6 1.7 bitcast_dynamic-update-slice_fusion.13
  7.3 1.7 bitcast_dynamic-update-slice_fusion.12
  9.0 1.7 bitcast_dynamic-update-slice_fusion.11
  10.7 1.7 bitcast_dynamic-update-slice_fusion.10
  12.3 1.7 bitcast_dynamic-update-slice_fusion.9
  14.0 1.7 bitcast_dynamic-update-slice_fusion.8
  15.7 1.7 bitcast_dynamic-update-slice_fusion.7
  17.4 1.7 bitcast_dynamic-update-slice_fusion.6
  19.1 1.7 bitcast_dynamic-update-slice_fusion.5
  20.7 1.7 bitcast_dynamic-update-slice_fusion.4
  22.4 1.7 bitcast_dynamic-update-slice_fusion.3
  24.1 1.7 bitcast_dynamic-update-slice_fusion.2
  25.7 1.7 bitcast_dynamic-update-slice_fusion.1
  27.4 7.4 %all-to-all-start = ((bf16[16,32,4096]{2,1,0:T(8,128)(2,1)}), bf16[16,32,4096]{2,1,0:T(8,128)(2,1)}, u32[]{:S(2)}, u32[]{:S(2)}) async-start(bf16[16,32,4096]{2,1,0:T(8,128)(2,1)} %bitcast_dynamic-update-slice_fusion.1), calls=%async_computation | async-start | bytes 8388608 | tf_op jit(solution)/shard_map/gradient_exchange/all_to_all | solution.py:42
  34.9 77.7 %all-to-all-done = bf16[16,32,4096]{2,1,0:T(8,128)(2,1)} async-done(((bf16[16,32,4096]{2,1,0:T(8,128)(2,1)}), bf16[16,32,4096]{2,1,0:T(8,128)(2,1)}, u32[]{:S(2)}, u32[]{:S(2)}) %all-to-all-start) | async-done | bytes 4194336 | tf_op jit(solution)/shard_map/gradient_exchange/all_to_all | solution.py:42
  112.5 8.1 %fusion = f32[8,2,32,1024]{3,2,1,0:T(8,128)S(1)} fusion(bf16[8,2,32,4096]{3,2,1,0:T(8,128)(2,1)} %bitcast.16, bf16[4096,1024]{1,0:T(8,128)(2,1)} %param.5), kind=kOutput, calls=%fused_computation.2 | convolution fusion | flops 4294967296 | bytes 14680064 | tf_op jit(solution)/shard_map/partial_projection/dot_general | solution.py:46
  120.8 0.8 collective-permute-start
  121.6 2.4 collective-permute-done
  124.0 1.4 bitcast_add_fusion
  125.5 6.3 %collective-permute-start.1 = (f32[4,32,1024]{2,1,0:T(8,128)S(1)}, f32[4,32,1024]{2,1,0:T(8,128)S(1)}, u32[]{:S(2)}, u32[]{:S(2)}) collective-permute-start(f32[4,32,1024]{2,1,0:T(8,128)S(1)} %dynamic-slice_bitcast_fusion.1), channel_id=1, source_target_pairs={{0,2},{1,3},{2,0},{3,1},{4,6},{5,7},{6,4},{7,5},{8,10},{9,11},{10,... | collective-permute-start | bytes 1572872 | tf_op jit(solution)/shard_map/sketch_reduce/ppermute | solution.py:8
  131.7 12.4 %collective-permute-done.1 = f32[4,32,1024]{2,1,0:T(8,128)S(1)} collective-permute-done((f32[4,32,1024]{2,1,0:T(8,128)S(1)}, f32[4,32,1024]{2,1,0:T(8,128)S(1)}, u32[]{:S(2)}, u32[]{:S(2)}) %collective-permute-start.1) | collective-permute-done | bytes 524320 | tf_op jit(solution)/shard_map/sketch_reduce/ppermute | solution.py:8
  144.3 11.4 %collective-permute-start.2 = (f32[2,32,1024]{2,1,0:T(8,128)S(1)}, f32[2,32,1024]{2,1,0:T(8,128)S(1)}, u32[]{:S(2)}, u32[]{:S(2)}) collective-permute-start(f32[2,32,1024]{2,1,0:T(8,128)S(1)} %dynamic-slice_bitcast_fusion.2), channel_id=1, source_target_pairs={{0,4},{1,5},{2,6},{3,7},{4,0},{5,1},{6,2},{7,3},{8,12},{9,13},{10,... | collective-permute-start | bytes 786440 | tf_op jit(solution)/shard_map/sketch_reduce/ppermute | solution.py:8
  155.7 6.3 %collective-permute-done.2 = f32[2,32,1024]{2,1,0:T(8,128)S(1)} collective-permute-done((f32[2,32,1024]{2,1,0:T(8,128)S(1)}, f32[2,32,1024]{2,1,0:T(8,128)S(1)}, u32[]{:S(2)}, u32[]{:S(2)}) %collective-permute-start.2) | collective-permute-done | bytes 262176 | tf_op jit(solution)/shard_map/sketch_reduce/ppermute | solution.py:8
  162.0 2.7 collective-permute-start.3
  164.7 5.7 %collective-permute-done.3 = f32[1,32,1024]{2,1,0:T(8,128)S(1)} collective-permute-done((f32[1,32,1024]{2,1,0:T(8,128)S(1)}, f32[1,32,1024]{2,1,0:T(8,128)S(1)}, u32[]{:S(2)}, u32[]{:S(2)}) %collective-permute-start.3) | collective-permute-done | bytes 131104 | tf_op jit(solution)/shard_map/sketch_reduce/ppermute | solution.py:8
  170.5 0.3 collective-permute-start.4
  170.8 7.9 %collective-permute-done.4 = f32[1,32,1024]{2,1,0:T(8,128)S(1)} collective-permute-done((f32[1,32,1024]{2,1,0:T(8,128)S(1)}, f32[1,32,1024]{2,1,0:T(8,128)S(1)}, u32[]{:S(2)}, u32[]{:S(2)}) %collective-permute-start.4) | collective-permute-done | bytes 131104 | tf_op jit(solution)/shard_map/sketch_gather/ppermute | solution.py:8
  178.8 8.2 %collective-permute-done.5 = f32[2,32,1024]{2,1,0:T(8,128)S(1)} collective-permute-done((f32[2,32,1024]{2,1,0:T(8,128)S(1)}, f32[2,32,1024]{2,1,0:T(8,128)S(1)}, u32[]{:S(2)}, u32[]{:S(2)}) %collective-permute-start.5) | collective-permute-done | bytes 262176 | tf_op jit(solution)/shard_map/sketch_gather/ppermute | solution.py:8
  187.2 13.0 %collective-permute-done.6 = f32[4,32,1024]{2,1,0:T(8,128)S(1)} collective-permute-done((f32[4,32,1024]{2,1,0:T(8,128)S(1)}, f32[4,32,1024]{2,1,0:T(8,128)S(1)}, u32[]{:S(2)}, u32[]{:S(2)}) %collective-permute-start.6) | collective-permute-done | bytes 524320 | tf_op jit(solution)/shard_map/sketch_gather/ppermute | solution.py:8
  200.7 2.0 convert_reduce_fusion
  202.8 0.4 collective-permute-done.7
  204.0 3.5 %fusion.61 = f32[512,512]{1,0:T(8,128)S(1)} fusion(f32[512,1024]{1,0:T(8,128)S(1)} %bitcast.144), kind=kOutput, calls=%fused_computation.142 | convolution fusion | flops 3221225472 | bytes 3145728 | tf_op jit(solution)/shard_map/kernel_matrix/dot_general | solution.py:62
  207.6 0.3 copy.18
  208.2 11.7 %cholesky.103 = f32[128,128]{1,0:T(8,128)S(1)} custom-call(f32[128,128]{1,0:T(8,128)S(1)} %cholesky.263), custom_call_target="Cholesky" | custom-call | tf_op jit(solution)/shard_map/kernel_solve/jit(cholesky)/cholesky | solution.py:65
  220.1 9.8 %custom-call.32 = f32[1,128,128]{1,2,0:T(8,128)S(1)} custom-call(f32[1,128,128]{2,1,0:T(8,128)S(1)} %get-tuple-element.37), custom_call_target="InvertDiagBlocksLowerTriangular" | custom-call | tf_op jit(solution)/shard_map/kernel_solve/jit(cholesky)/cholesky | solution.py:65
  229.9 0.3 constant_dynamic-update-slice_fusion
  230.2 0.3 convolution_subtract_fusion
  230.6 11.9 %cholesky.215 = f32[128,128]{1,0:T(8,128)S(1)} custom-call(f32[128,128]{1,0:T(8,128)S(1)} %cholesky.267), custom_call_target="Cholesky" | custom-call | tf_op jit(solution)/shard_map/kernel_solve/jit(cholesky)/cholesky | solution.py:65
  242.5 9.8 %custom-call.33 = f32[1,128,128]{1,2,0:T(8,128)S(1)} custom-call(f32[1,128,128]{2,1,0:T(8,128)S(1)} %get-tuple-element.34), custom_call_target="InvertDiagBlocksLowerTriangular" | custom-call | tf_op jit(solution)/shard_map/kernel_solve/jit(cholesky)/cholesky | solution.py:65
  252.3 0.3 convolution_dynamic-update-slice_fusion
  252.6 0.4 convolution_subtract_fusion.1
  253.0 11.7 %cholesky.236 = f32[128,128]{1,0:T(8,128)S(1)} custom-call(f32[128,128]{1,0:T(8,128)S(1)} %cholesky.272), custom_call_target="Cholesky" | custom-call | tf_op jit(solution)/shard_map/kernel_solve/jit(cholesky)/cholesky | solution.py:65
  264.7 9.8 %custom-call.34 = f32[1,128,128]{1,2,0:T(8,128)S(1)} custom-call(f32[1,128,128]{2,1,0:T(8,128)S(1)} %get-tuple-element.31), custom_call_target="InvertDiagBlocksLowerTriangular" | custom-call | tf_op jit(solution)/shard_map/kernel_solve/jit(cholesky)/cholesky | solution.py:65
  274.8 0.6 convolution_subtract_fusion.2
  275.4 11.7 %cholesky.253 = f32[128,128]{1,0:T(8,128)S(1)} custom-call(f32[128,128]{1,0:T(8,128)S(1)} %convolution_subtract_fusion.2), custom_call_target="Cholesky" | custom-call | tf_op jit(solution)/shard_map/kernel_solve/jit(cholesky)/cholesky | solution.py:65
  287.1 0.7 compare_reduce_fusion.1
  287.8 0.7 compare_reduce_fusion
  288.5 0.7 compare_reduce_fusion.2
  291.8 10.5 %while.1 = (s32[]{:T(128)}, f32[512,512]{1,0:T(8,128)S(1)}, s32[4,2]{0,1:T(2,128)S(1)}, f32[4,128,128]{2,1,0:T(8,128)}, s32[]{:T(128)}) while((s32[]{:T(128)}, f32[512,512]{1,0:T(8,128)S(1)}, s32[4,2]{0,1:T(2,128)S(1)}, f32[4,128,128]{2,1,0:T(8,128)}, s32[]{:T(128)}) %tuple.35), condition=%wide.while_cond, body=%wide.while_body.sunk | while | flops 2 | bytes 132205 | solution.py:67
  291.9 0.6 fusion.76
  292.5 2.0 bitcast_dynamic-update-slice_fusion.18
  294.5 0.6 fusion.76
  295.1 2.0 bitcast_dynamic-update-slice_fusion.18
  297.2 0.6 fusion.76
  297.7 2.0 bitcast_dynamic-update-slice_fusion.18
  299.8 0.6 fusion.76
  300.4 2.0 bitcast_dynamic-update-slice_fusion.18
  302.3 40.1 %custom-call.35 = f32[4,128,128]{1,2,0:T(8,128)S(1)} custom-call(f32[4,128,128]{2,1,0:T(8,128)} %get-tuple-element.9), custom_call_target="InvertDiagBlocksLowerTriangular" | custom-call | tf_op jit(solution)/shard_map/kernel_solve/triangular_solve | solution.py:67
  343.4 0.3 convolution_subtract_fusion.6
  345.0 0.3 convolution_subtract_fusion.3
  345.5 0.8 fusion.20
  (60 shorter events, 5.4 us)
Async XLA Ops:
  27.4 85.1 %all-to-all-start = ((bf16[16,32,4096]{2,1,0:T(8,128)(2,1)}), bf16[16,32,4096]{2,1,0:T(8,128)(2,1)}, u32[]{:S(2)}, u32[]{:S(2)}) async-start(bf16[16,32,4096]{2,1,0:T(8,128)(2,1)} %bitcast_dynamic-update-slice_fusion.1), calls=%async_computation | async-start | bytes 8388608 | tf_op jit(solution)/shard_map/gradient_exchange/all_to_all | solution.py:42
  120.8 3.3 collective-permute-start
  125.5 18.7 %collective-permute-start.1 = (f32[4,32,1024]{2,1,0:T(8,128)S(1)}, f32[4,32,1024]{2,1,0:T(8,128)S(1)}, u32[]{:S(2)}, u32[]{:S(2)}) collective-permute-start(f32[4,32,1024]{2,1,0:T(8,128)S(1)} %dynamic-slice_bitcast_fusion.1), channel_id=1, source_target_pairs={{0,2},{1,3},{2,0},{3,1},{4,6},{5,7},{6,4},{7,5},{8,10},{9,11},{10,... | collective-permute-start | bytes 1572872 | tf_op jit(solution)/shard_map/sketch_reduce/ppermute | solution.py:8
  144.3 17.7 %collective-permute-start.2 = (f32[2,32,1024]{2,1,0:T(8,128)S(1)}, f32[2,32,1024]{2,1,0:T(8,128)S(1)}, u32[]{:S(2)}, u32[]{:S(2)}) collective-permute-start(f32[2,32,1024]{2,1,0:T(8,128)S(1)} %dynamic-slice_bitcast_fusion.2), channel_id=1, source_target_pairs={{0,4},{1,5},{2,6},{3,7},{4,0},{5,1},{6,2},{7,3},{8,12},{9,13},{10,... | collective-permute-start | bytes 786440 | tf_op jit(solution)/shard_map/sketch_reduce/ppermute | solution.py:8
  162.0 8.4 %collective-permute-start.3 = (f32[1,32,1024]{2,1,0:T(8,128)S(1)}, f32[1,32,1024]{2,1,0:T(8,128)S(1)}, u32[]{:S(2)}, u32[]{:S(2)}) collective-permute-start(f32[1,32,1024]{2,1,0:T(8,128)S(1)} %constant_dynamic-slice_fusion.1), channel_id=1, source_target_pairs={{0,8},{1,9},{2,10},{3,11},{4,12},{5,13},{6,14},{7,15},{8,0},{9,1},... | collective-permute-start | bytes 393224 | tf_op jit(solution)/shard_map/sketch_reduce/ppermute | solution.py:8
  170.5 30.0 %copy-start = (f32[1,32,1024]{2,1,0:T(8,128)}, f32[1,32,1024]{2,1,0:T(8,128)S(1)}, u32[]{:S(2)}) copy-start(f32[1,32,1024]{2,1,0:T(8,128)S(1)} %dynamic-slice_add_fusion) | copy-start | bytes 393220
  170.5 8.2 %collective-permute-start.4 = (f32[1,32,1024]{2,1,0:T(8,128)S(1)}, f32[1,32,1024]{2,1,0:T(8,128)S(1)}, u32[]{:S(2)}, u32[]{:S(2)}) collective-permute-start(f32[1,32,1024]{2,1,0:T(8,128)S(1)} %dynamic-slice_add_fusion), channel_id=1, source_target_pairs={{0,8},{1,9},{2,10},{3,11},{4,12},{5,13},{6,14},{7,15},{8,0},{9,1},... | collective-permute-start | bytes 393224 | tf_op jit(solution)/shard_map/sketch_gather/ppermute | solution.py:8
  178.7 8.3 %collective-permute-start.5 = (f32[2,32,1024]{2,1,0:T(8,128)S(1)}, f32[2,32,1024]{2,1,0:T(8,128)S(1)}, u32[]{:S(2)}, u32[]{:S(2)}) collective-permute-start(f32[2,32,1024]{2,1,0:T(8,128)S(1)} %maximum_bitcast_fusion), channel_id=1, source_target_pairs={{0,4},{1,5},{2,6},{3,7},{4,0},{5,1},{6,2},{7,3},{8,12},{9,13},{10,... | collective-permute-start | bytes 786440 | tf_op jit(solution)/shard_map/sketch_gather/ppermute | solution.py:8
  178.8 21.8 %copy-start.2 = (s32[24]{0:T(128)S(1)}, s32[24]{0:T(128)}, u32[]{:S(2)}) copy-start(s32[24]{0:T(128)} %param.7) | copy-start | bytes 292
  178.8 21.9 %copy-start.1 = (s32[24,128]{1,0:T(8,128)S(1)}, s32[24,128]{1,0:T(8,128)}, u32[]{:S(2)}) copy-start(s32[24,128]{1,0:T(8,128)} %param.6) | copy-start | bytes 36868
  187.1 13.1 %collective-permute-start.6 = (f32[4,32,1024]{2,1,0:T(8,128)S(1)}, f32[4,32,1024]{2,1,0:T(8,128)S(1)}, u32[]{:S(2)}, u32[]{:S(2)}) collective-permute-start(f32[4,32,1024]{2,1,0:T(8,128)S(1)} %bitcast.148), channel_id=1, source_target_pairs={{0,2},{1,3},{2,0},{3,1},{4,6},{5,7},{6,4},{7,5},{8,10},{9,11},{10,... | collective-permute-start | bytes 1572872 | tf_op jit(solution)/shard_map/sketch_gather/ppermute | solution.py:8
  200.5 2.7 collective-permute-start.7
